TPU v7x, 32 devices: a whole 2x2x4 slice. The times are simulated.
32 devices in a mesh: grp: 4 (over z), exp: 8 (over y, x, core).
Axes of the slice: x: 2, y: 2, z: 4, core: 2. Of those that a mesh axis runs over, the one named last changes fastest.
Arguments:
- cotangent: bfloat16 [4096, 1440], P(('grp', 'exp')), may hold values from -6 to 6
- hidden: bfloat16 [4096, 4, 1440], P(('grp', 'exp')), may hold values from -0.29882812 to 0.29882812
- gates: bfloat16 [4096, 4], P(('grp', 'exp')), may hold values from 0.049804688 to 1
- expert_ids: int32 [4096, 4], P(('grp', 'exp')), may hold values from 0 to 15, all different within a row; in each aligned block of 128 rows (0 to 127, 128 to 255, ...) at most 40 rows name the same one
- group_counts: int32 [4], P('grp'), may hold values from 146 to 1024, as said below
- w_down: bfloat16 [16, 1440, 1440], P('exp', 'grp'), may hold values from -0.15625 to 0.15625
Outputs:
- d_hidden: bfloat16 [4096, 4, 1440], P(('grp', 'exp'))
- d_gate: bfloat16 [4096, 4], P(('grp', 'exp'))
- d_weight: float32 [16, 1440, 1440], P('exp', 'grp')
Inputs may be any that keep to these rules, and one draw needn't show every extreme that they name: `expert_ids`: within the rows of one device no expert is named more than 40 times, and every expert is named somewhere. `group_counts`: some group has all 1024 slots live, and some group only 146.
All inputs are finite; a program needn't handle non-finite values.
Results may differ from a plain program's by a relative error of at most 0.015.
Values may be sent and summed in bfloat16 or wider, within the bound.
No kernel may reach another device: no remote copies, remote signals or barrier semaphores. Data moves between devices by JAX's collectives and lax.ppermute only.
A program may use at most 128 MiB of HBM per device.

v0:
```python
import jax
import jax.numpy as jnp
from jax import lax
from jax.sharding import PartitionSpec as P

LOSS_SCALE = 32768


def body(cotangent, hidden, gates, expert_ids, group_counts, w_down):
    tok = cotangent.shape[0]
    top = expert_ids.shape[1]
    ffw = hidden.shape[2]
    width = cotangent.shape[1]
    n_exp = lax.axis_size("exp")
    exp_dev = w_down.shape[0]
    experts = exp_dev * n_exp
    most = 5 * tok * top // (4 * experts)
    count = group_counts[0]
    first_row = lax.axis_index("exp") * tok
    live = (first_row + jnp.arange(tok, dtype=jnp.int32) < count).astype(jnp.float32)
    total = lax.psum(count.astype(jnp.float32), "grp")
    scale = LOSS_SCALE / total
    weighted = (gates.astype(jnp.float32) * live[:, None]).astype(jnp.bfloat16)
    flat_ids = expert_ids.reshape(-1)
    onehot = (flat_ids[:, None] == jnp.arange(experts, dtype=jnp.int32)[None, :]).astype(jnp.int32)
    rank = jnp.sum((jnp.cumsum(onehot, axis=0) - onehot) * onehot, axis=1)
    target = flat_ids * most + rank
    slot_tok = jnp.arange(tok * top, dtype=jnp.int32) // top
    dy_buf = jnp.zeros((experts * most, width), jnp.bfloat16).at[target].set(cotangent[slot_tok])
    hid_buf = jnp.zeros((experts * most, ffw), jnp.bfloat16).at[target].set(hidden.reshape(-1, ffw))
    gate_buf = jnp.zeros((experts * most,), jnp.bfloat16).at[target].set(weighted.reshape(-1))
    dy_buf = dy_buf.reshape(n_exp, exp_dev * most, width)
    hid_buf = hid_buf.reshape(n_exp, exp_dev * most, ffw)
    gate_buf = gate_buf.reshape(n_exp, exp_dev * most)
    dy_recv, gate_recv = (
        lax.all_to_all(dy_buf, "exp", split_axis=0, concat_axis=0, tiled=True),
        lax.all_to_all(gate_buf, "exp", split_axis=0, concat_axis=0, tiled=True),
    )
    hid_recv = lax.all_to_all(hid_buf, "exp", split_axis=0, concat_axis=0, tiled=True)
    dy_four = dy_recv.reshape(n_exp, exp_dev, most, width)
    hid_four = hid_recv.reshape(n_exp, exp_dev, most, ffw)
    gate_three = gate_recv.reshape(n_exp, exp_dev, most).astype(jnp.float32)
    proj = jnp.einsum(
        "sjmd,jfd->sjmf",
        dy_four,
        lax.all_gather(w_down, "grp", axis=1, tiled=True),
        preferred_element_type=jnp.float32,
    )
    dh_rows = (gate_three[..., None] * proj).astype(jnp.bfloat16)
    inner = jnp.sum(hid_four.astype(jnp.float32) * proj, axis=3).astype(jnp.bfloat16)
    scaled = (gate_three[..., None] * dy_four.astype(jnp.float32)).astype(jnp.bfloat16)
    partial_grad = (
        jnp.einsum("sjmf,sjmd->jfd", hid_four, scaled, preferred_element_type=jnp.float32) * scale
    )
    d_weight = lax.psum_scatter(
        partial_grad.astype(jnp.bfloat16), "grp", scatter_dimension=1, tiled=True
    ).astype(jnp.float32)
    back_dh, back_inner = (
        lax.all_to_all(
            dh_rows.reshape(n_exp, exp_dev * most, ffw),
            "exp",
            split_axis=0,
            concat_axis=0,
            tiled=True,
        ),
        lax.all_to_all(
            inner.reshape(n_exp, exp_dev * most), "exp", split_axis=0, concat_axis=0, tiled=True
        ),
    )
    d_hidden = back_dh.reshape(experts * most, ffw)[target].reshape(tok, top, ffw)
    inner_tok = back_inner.reshape(-1)[target].reshape(tok, top)
    d_gate = (inner_tok.astype(jnp.float32) * live[:, None]).astype(jnp.bfloat16)
    return (d_hidden, d_gate, d_weight)


def solution(mesh):
    in_specs = (
        P(("grp", "exp"), None),
        P(("grp", "exp"), None, None),
        P(("grp", "exp"), None),
        P(("grp", "exp"), None),
        P("grp"),
        P("exp", "grp", None),
    )
    out_specs = (P(("grp", "exp"), None, None), P(("grp", "exp"), None), P("exp", "grp", None))
    return jax.shard_map(body, mesh=mesh, in_specs=in_specs, out_specs=out_specs, check_vma=False)
```

profile of v0, /device:TPU:0, one launch (start us, length us, event | category | flops | bytes accessed | tf_op | source)
XLA Modules:
  0.0 501.5 jit_solution(16202728035999669125)
XLA Ops:
  8.5 1.2 reduce-window.6
  11.0 3.8 scatter_custom_fusion
  15.5 5.2 %all-to-all-start = ((bf16[8,1,80]{2,1,0:T(2,128)(2,1)}), bf16[8,1,80]{2,1,0:T(2,128)(2,1)S(1)}, u32[]{:S(2)}, u32[]{:S(2)}) async-start(bf16[8,1,80]{2,1,0:T(2,128)(2,1)} %all_to_all.25), calls=%async_computation | async-start | bytes 8192 | tf_op jit(solution)/shard_map/all_to_all | solution.py:37
  20.6 1.6 copy.55
  23.0 4.5 scatter_custom_fusion.2
  27.5 4.3 all-to-all-start.3
  32.0 9.6 %scatter_custom_fusion.1 = bf16[640,1440]{1,0:T(8,128)(2,1)} fusion(s32[512]{0:T(512)S(1)} %bitcast.59, bf16[128,1440]{1,0:T(8,128)(2,1)S(1)} %copy.52, s32[1024]{0:T(1024)S(1)} %pad_clamp_fusion.1, bf16[]{:T(256)} %constant.15.clone.1), kind=kCustom, calls=%fused_computation.18 | custom fusion | bytes 1843202 | tf_op jit(solution)/shard_map/scatter | solution.py:29
  41.6 15.5 %all-to-all-done.3 = bf16[8,80,1440]{2,1,0:T(8,128)(2,1)S(1)} async-done(((bf16[8,80,1440]{2,1,0:T(8,128)(2,1)}), bf16[8,80,1440]{2,1,0:T(8,128)(2,1)S(1)}, u32[]{:S(2)}, u32[]{:S(2)}) %all-to-all-start.3) | async-done | bytes 1843232 | tf_op jit(solution)/shard_map/all_to_all | solution.py:39
  57.0 4.3 all-to-all-start.1
  61.4 15.4 %psum.7 = f32[]{:T(128)} all-reduce(f32[]{:T(128)S(6)} %convert_element_type.90), channel_id=1, replica_groups=mesh['grp'=4,'exp'=8] {'grp'}, use_global_device_ids=true, to_apply=%region_7.8 | all-reduce | flops 1 | bytes 8 | tf_op jit(solution)/shard_map/psum | solution.py:21
  77.6 9.0 %all-to-all-done.1 = bf16[8,80,1440]{2,1,0:T(8,128)(2,1)} async-done(((bf16[8,80,1440]{2,1,0:T(8,128)(2,1)}), bf16[8,80,1440]{2,1,0:T(8,128)(2,1)}, u32[]{:S(2)}, u32[]{:S(2)}) %all-to-all-start.1) | async-done | bytes 1843232 | tf_op jit(solution)/shard_map/all_to_all | solution.py:36
  86.6 83.1 %all-gather.2.cloned.1.call-done = bf16[2,1440,1440]{2,1,0:T(8,128)(2,1)} async-done(((bf16[2,360,1440]{2,1,0:T(8,128)(2,1)}), bf16[2,1440,1440]{2,1,0:T(8,128)(2,1)}) %all-gather.2.cloned.1.call-update) | async-done | bytes 8294416 | tf_op jit(solution)/shard_map/all_gather | solution.py:46
  169.7 9.6 %fusion.4 = (bf16[8,2,40]{2,0,1:T(8,128)(2,1)S(1)}, bf16[8,2,40,1440]{3,2,0,1:T(8,128)(2,1)}, bf16[8,2,40,1440]{3,2,0,1:T(8,128)(2,1)S(1)}) fusion(bf16[8,2,40,1440]{3,2,1,0:T(8,128)(2,1)S(1)} %bitcast.55, f32[8,2,40]{2,0,1:T(8,128)S(1)} %copy.51, bf16[8,2,40,1440]{3,2,1,0:T(8,128)(2,1)} %bitcast.6, bf16[2,1440,1440]{2,1,0:T(8,128)(2,1)} %all-gather.2.cloned.1.call-done), kind=kOutput, calls=%fused_computation.13 | convolution fusion | flops 2661580288 | bytes 15671040 | tf_op jit(solution)/shard_map/sjmd,jfd->sjmf/dot_general | solution.py:43
  179.3 7.1 %fusion = bf16[2,1440,1440]{2,1,0:T(8,128)(2,1)} fusion(bf16[8,2,40,1440]{3,2,1,0:T(8,128)(2,1)S(1)} %bitcast.56, f32[]{:T(128)S(6)} %div.13, bf16[8,2,40,1440]{3,2,0,1:T(8,128)(2,1)S(1)} %get-tuple-element.17), kind=kOutput, calls=%fused_computation.7 | convolution fusion | flops 2662502400 | bytes 11980804 | tf_op jit(solution)/shard_map/sjmf,sjmd->jfd/dot_general | solution.py:53
  187.0 3.7 all-to-all-start.4
  190.7 1.5 copy.54
  192.1 3.1 all-to-all-done.4
  195.3 3.7 all-to-all-start.2
  200.4 3.5 gather_fusion.1
  204.8 19.4 %all-to-all-done.2 = bf16[8,80,1440]{2,1,0:T(8,128)(2,1)S(1)} async-done(((bf16[8,80,1440]{2,1,0:T(8,128)(2,1)}), bf16[8,80,1440]{2,1,0:T(8,128)(2,1)S(1)}, u32[]{:S(2)}, u32[]{:S(2)}) %all-to-all-start.2) | async-done | bytes 1843232 | tf_op jit(solution)/shard_map/all_to_all | solution.py:59
  224.2 2.1 gather_fusion
  226.7 2.4 copy.61
  229.2 261.2 %all-reduce.3.cloned.1.call-done = bf16[2,1440,1440]{2,1,0:T(8,128)(2,1)} async-done(((bf16[2,1440,1440]{2,1,0:T(8,128)(2,1)}), bf16[2,1440,1440]{2,1,0:T(8,128)(2,1)}) %all-reduce.3.cloned.1.call-update) | async-done | bytes 8294416
  490.3 4.3 dynamic-slice_convert_fusion
  (51 shorter events, 6.4 us)
Async XLA Ops:
  7.2 0.8 copy-start.3
  7.2 3.4 copy-start.4
  7.2 13.4 %copy-start.1 = (bf16[128,4,1440]{0,2,1:T(8,128)(2,1)S(1)}, bf16[128,4,1440]{0,2,1:T(8,128)(2,1)}, u32[]{:S(2)}) copy-start(bf16[128,4,1440]{0,2,1:T(8,128)(2,1)} %param.7) | copy-start | bytes 4423684
  7.2 162.5 %all-gather.2.cloned.1.call-start = ((), (), s32[]{:S(2)}) async-start(), calls=%async_computation.5 | async-start | bytes 11059200 | tf_op jit(solution)/shard_map/all_gather | solution.py:46
  15.5 12.0 %all-to-all-start = ((bf16[8,1,80]{2,1,0:T(2,128)(2,1)}), bf16[8,1,80]{2,1,0:T(2,128)(2,1)S(1)}, u32[]{:S(2)}, u32[]{:S(2)}) async-start(bf16[8,1,80]{2,1,0:T(2,128)(2,1)} %all_to_all.25), calls=%async_computation | async-start | bytes 8192 | tf_op jit(solution)/shard_map/all_to_all | solution.py:37
  27.5 4.3 copy-start.2
  27.5 29.6 %all-to-all-start.3 = ((bf16[8,80,1440]{2,1,0:T(8,128)(2,1)}), bf16[8,80,1440]{2,1,0:T(8,128)(2,1)S(1)}, u32[]{:S(2)}, u32[]{:S(2)}) async-start(bf16[8,80,1440]{2,1,0:T(8,128)(2,1)} %bitcast.12), calls=%async_computation.3 | async-start | bytes 3932160 | tf_op jit(solution)/shard_map/all_to_all | solution.py:39
  57.0 29.6 %all-to-all-start.1 = ((bf16[8,80,1440]{2,1,0:T(8,128)(2,1)}), bf16[8,80,1440]{2,1,0:T(8,128)(2,1)}, u32[]{:S(2)}, u32[]{:S(2)}) async-start(bf16[8,80,1440]{2,1,0:T(8,128)(2,1)} %bitcast.5), calls=%async_computation.1 | async-start | bytes 3932160 | tf_op jit(solution)/shard_map/all_to_all | solution.py:36
  61.4 429.0 %all-reduce.3.cloned.1.call-start = ((), (), s32[]{:S(2)}) async-start(), calls=%async_computation.6 | async-start | bytes 17694720
  186.3 4.4 copy-start
  187.0 8.2 %all-to-all-start.4 = ((bf16[8,1,80]{2,1,0:T(2,128)(2,1)}), bf16[8,1,80]{2,1,0:T(2,128)(2,1)S(1)}, u32[]{:S(2)}, u32[]{:S(2)}) async-start(bf16[8,1,80]{2,1,0:T(2,128)(2,1)} %convert_element_type.95), calls=%async_computation.4 | async-start | bytes 8192 | tf_op jit(solution)/shard_map/all_to_all | solution.py:66
  195.3 3.7 copy-start.5
  195.3 28.9 %all-to-all-start.2 = ((bf16[8,80,1440]{2,1,0:T(8,128)(2,1)}), bf16[8,80,1440]{2,1,0:T(8,128)(2,1)S(1)}, u32[]{:S(2)}, u32[]{:S(2)}) async-start(bf16[8,80,1440]{2,1,0:T(8,128)(2,1)} %bitcast.54), calls=%async_computation.2 | async-start | bytes 3932160 | tf_op jit(solution)/shard_map/all_to_all | solution.py:59
Sparse Core Ops, SparseCore 0:
  9.6 160.0 all-gather.1
  186.5 303.8 all-reduce.2
where the time goes:
time: 502 us; the launch traced here: 501 us
  waiting for transfers between devices  392 us (78%)
  local copies, waits for them, and re-layouts  34.2 us (7%)
  starting transfers between devices  21.3 us (4%)
  matrix products  16.6 us (3%)
  between operations  16.3 us (3%)
  blocking collectives  15.4 us (3%)
  other arithmetic  5.77 us (1%)
    unnamed x3, waiting for transfers between devices  262 us
    all_gather x1, waiting for transfers between devices, body(): lax.all_gather(w_down, 'grp', axis=1, tiled=True)  83.1 us
    all_to_all x1, waiting for transfers between devices, body(): lax.all_to_all(dh_rows.reshape(n_exp, exp_dev * most, ffw), 'exp', split_...  19.4 us
    all_to_all x1, waiting for transfers between devices, body(): lax.all_to_all(hid_buf, 'exp', split_axis=0, concat_axis=0, tiled=True)  15.5 us
    psum x1, blocking collectives, body(): total = lax.psum(count.astype(jnp.float32), 'grp')  15.4 us
  transfers between devices with their start and end apart: 7, of which 6 were waited for; matrix products, arithmetic and copies ran while one was open for 7% of the time, Pallas kernels for 0%

commit v1 on v0

--- a/solution.py
+++ b/solution.py
@@ -4,6 +4,18 @@
 from jax.sharding import PartitionSpec as P
 
 LOSS_SCALE = 32768
+
+
+def doubled_up(x, axis, dim):
+    ways, here, lap = (lax.axis_size(axis), lax.axis_index(axis), x.shape[dim])
+    line, have = (x, 1)
+    while have < ways:
+        line = jnp.concatenate(
+            [line, lax.ppermute(line, axis, [(d, (d - have) % ways) for d in range(ways)])],
+            axis=dim,
+        )
+        have = 2 * have
+    return jnp.roll(line, here * lap, axis=dim)
 
 
 def body(cotangent, hidden, gates, expert_ids, group_counts, w_down):
@@ -41,10 +53,7 @@
     hid_four = hid_recv.reshape(n_exp, exp_dev, most, ffw)
     gate_three = gate_recv.reshape(n_exp, exp_dev, most).astype(jnp.float32)
     proj = jnp.einsum(
-        "sjmd,jfd->sjmf",
-        dy_four,
-        lax.all_gather(w_down, "grp", axis=1, tiled=True),
-        preferred_element_type=jnp.float32,
+        "sjmd,jfd->sjmf", dy_four, doubled_up(w_down, "grp", 1), preferred_element_type=jnp.float32
     )
     dh_rows = (gate_three[..., None] * proj).astype(jnp.bfloat16)
     inner = jnp.sum(hid_four.astype(jnp.float32) * proj, axis=3).astype(jnp.bfloat16)

time: 502 us -> 638 us (1.27)
  blocking collectives: 15.4 us -> 78.1 us
  waiting for transfers between devices: 392 us -> 433 us
  local copies, waits for them, and re-layouts: 34.2 us -> 52.2 us
    ppermute x0 -> x2, waiting for transfers between devices: none -> 118 us  [doubled_up(): lax.ppermute(line, axis, [(d, (d - have) % ways) for d in range(ways)])]
    all_gather x1 -> x0, waiting for transfers between devices: 83.1 us -> none  [body(): lax.all_gather(w_down, 'grp', axis=1, tiled=True)]
    psum x1, blocking collectives: 15.4 us -> 78.1 us  [body(): total = lax.psum(count.astype(jnp.float32), 'grp')]
    unnamed x3 -> x2, waiting for transfers between devices: 262 us -> 292 us
    all_to_all x1, waiting for transfers between devices: 15.5 us -> 0.01 us  [body(): lax.all_to_all(hid_buf, 'exp', split_axis=0, concat_axis=0, tiled=True)]
    unnamed x18 -> x27, local copies, waits for them, and re-layouts: 5.58 us -> 18.9 us
    all_to_all x1, waiting for transfers between devices: 9.02 us -> 0.01 us  [body(): lax.all_to_all(dy_buf, 'exp', split_axis=0, concat_axis=0, tiled=True)]
    ppermute x0 -> x2, starting transfers between devices: none -> 6.47 us  [doubled_up(): lax.ppermute(line, axis, [(d, (d - have) % ways) for d in range(ways)])]
  transfers between devices with their start and end apart: 7 -> 8, of which waited for: 6 -> 5; matrix products, arithmetic and copies ran while one was open for 7% -> 8% of each run, Pallas kernels for 0% -> 0%
where the time goes in v1:
time: 638 us; the launch traced here: 637 us
  waiting for transfers between devices  433 us (68%)
  blocking collectives  78.1 us (12%)
  local copies, waits for them, and re-layouts  52.2 us (8%)
  starting transfers between devices  26.8 us (4%)
  matrix products  20.6 us (3%)
  between operations  16.3 us (3%)
  other arithmetic  10.7 us (2%)
    unnamed x2, waiting for transfers between devices  292 us
    ppermute x2, waiting for transfers between devices, doubled_up(): lax.ppermute(line, axis, [(d, (d - have) % ways) for d in range(ways)])  118 us
    psum x1, blocking collectives, body(): total = lax.psum(count.astype(jnp.float32), 'grp')  78.1 us
    all_to_all x1, waiting for transfers between devices, body(): lax.all_to_all(dh_rows.reshape(n_exp, exp_dev * most, ffw), 'exp', split_...  19.2 us
    unnamed x27, local copies, waits for them, and re-layouts  18.9 us
  transfers between devices with their start and end apart: 8, of which 5 were waited for; matrix products, arithmetic and copies ran while one was open for 8% of the time, Pallas kernels for 0%

profile of v1, /device:TPU:0, one launch (start us, length us, event | category | flops | bytes accessed | tf_op | source)
XLA Modules:
  0.0 637.4 jit_solution(16660515834725999849)
XLA Ops:
  7.2 5.1 collective-permute-start
  12.3 47.7 %collective-permute-done = bf16[2,360,1440]{2,1,0:T(8,128)(2,1)S(1)} collective-permute-done((bf16[2,360,1440]{2,1,0:T(8,128)(2,1)}, bf16[2,360,1440]{2,1,0:T(8,128)(2,1)S(1)}, u32[]{:S(2)}, u32[]{:S(2)}) %collective-permute-start) | collective-permute-done | bytes 2073632 | tf_op jit(solution)/shard_map/ppermute | solution.py:14
  60.0 4.9 pad_maximum_fusion
  69.3 3.8 scatter_custom_fusion
  73.7 3.7 all-to-all-start
  79.8 4.5 scatter_custom_fusion.2
  84.4 4.5 all-to-all-start.3
  88.9 78.1 %psum.7 = f32[]{:T(128)} all-reduce(f32[]{:T(128)S(6)} %convert_element_type.90), channel_id=1, replica_groups=mesh['grp'=4,'exp'=8] {'grp'}, use_global_device_ids=true, to_apply=%region_7.8 | all-reduce | flops 1 | bytes 8 | tf_op jit(solution)/shard_map/psum | solution.py:33
  167.2 9.6 %scatter_custom_fusion.1 = bf16[640,1440]{1,0:T(8,128)(2,1)} fusion(s32[512]{0:T(512)S(1)} %bitcast.58, bf16[128,1440]{1,0:T(8,128)(2,1)S(1)} %copy.52, s32[1024]{0:T(1024)S(1)} %pad_clamp_fusion.1, bf16[]{:T(256)} %constant.50.clone.1), kind=kCustom, calls=%fused_computation.20 | custom fusion | bytes 1843202 | tf_op jit(solution)/shard_map/scatter | solution.py:41
  179.2 4.3 all-to-all-start.1
  183.8 3.2 constant_dynamic-update-slice_fusion.4
  187.0 70.5 %collective-permute-done.1 = bf16[2,720,1440]{2,1,0:T(8,128)(2,1)} collective-permute-done((bf16[2,720,1440]{2,1,0:T(8,128)(2,1)}, bf16[2,720,1440]{2,1,0:T(8,128)(2,1)}, u32[]{:S(2)}, u32[]{:S(2)}) %collective-permute-start.1) | collective-permute-done | bytes 4147232 | tf_op jit(solution)/shard_map/ppermute | solution.py:14
  257.4 4.6 constant_dynamic-update-slice_fusion.3
  266.0 4.6 constant_dynamic-update-slice_fusion
  270.6 10.3 %fusion.5 = (bf16[8,2,40]{2,0,1:T(8,128)(2,1)S(1)}, bf16[8,2,40,1440]{3,2,0,1:T(8,128)(2,1)S(1)}, bf16[8,2,40,1440]{3,2,0,1:T(8,128)(2,1)}) fusion(bf16[8,2,40,1440]{3,2,1,0:T(8,128)(2,1)} %bitcast.13, f32[8,2,40]{2,0,1:T(8,128)S(1)} %copy.51, bf16[8,2,40,1440]{3,2,1,0:T(8,128)(2,1)} %bitcast.8, ...), kind=kOutput, calls=%fused_computation.15 | convolution fusion | flops 2661580288 | bytes 18435844 | tf_op jit(solution)/shard_map/sjmd,jfd->sjmf/dot_general | solution.py:55
  280.9 10.3 %fusion = bf16[2,1440,1440]{2,1,0:T(8,128)(2,1)} fusion(bf16[8,2,40,1440]{3,2,1,0:T(8,128)(2,1)} %bitcast.13, f32[]{:T(128)S(6)} %div.13, bf16[8,2,40,1440]{3,2,0,1:T(8,128)(2,1)} %get-tuple-element.17), kind=kOutput, calls=%fused_computation.7 | convolution fusion | flops 2662502400 | bytes 11980804 | tf_op jit(solution)/shard_map/sjmf,sjmd->jfd/dot_general | solution.py:62
  291.9 3.7 all-to-all-start.4
  297.1 3.1 all-to-all-done.4
  300.2 3.9 all-to-all-start.2
  305.5 3.5 gather_fusion.1
  309.9 19.2 %all-to-all-done.2 = bf16[8,80,1440]{2,1,0:T(8,128)(2,1)S(1)} async-done(((bf16[8,80,1440]{2,1,0:T(8,128)(2,1)}), bf16[8,80,1440]{2,1,0:T(8,128)(2,1)S(1)}, u32[]{:S(2)}, u32[]{:S(2)}) %all-to-all-start.2) | async-done | bytes 1843232 | tf_op jit(solution)/shard_map/all_to_all | solution.py:68
  331.6 2.4 copy.61
  334.0 292.2 %all-reduce.3.cloned.1.call-done = bf16[2,1440,1440]{2,1,0:T(8,128)(2,1)} async-done(((bf16[2,1440,1440]{2,1,0:T(8,128)(2,1)}), bf16[2,1440,1440]{2,1,0:T(8,128)(2,1)}) %all-reduce.3.cloned.1.call-update) | async-done | bytes 8294416
  626.3 4.3 dynamic-slice_convert_fusion
  (63 shorter events, 19.1 us)
Async XLA Ops:
  7.2 59.1 %copy-start.5 = (s32[128,4]{0,1:T(4,128)S(1)}, s32[128,4]{0,1:T(4,128)}, u32[]{:S(2)}) copy-start(s32[128,4]{0,1:T(4,128)} %param.9) | copy-start | bytes 6148
  7.2 61.7 %copy-start.6 = (bf16[128,4]{0,1:T(4,128)(2,1)S(1)}, bf16[128,4]{0,1:T(4,128)(2,1)}, u32[]{:S(2)}) copy-start(bf16[128,4]{0,1:T(4,128)(2,1)} %param.8) | copy-start | bytes 3076
  7.2 70.3 %copy-start.3 = (bf16[128,4,1440]{0,2,1:T(8,128)(2,1)S(1)}, bf16[128,4,1440]{0,2,1:T(8,128)(2,1)}, u32[]{:S(2)}) copy-start(bf16[128,4,1440]{0,2,1:T(8,128)(2,1)} %param.7) | copy-start | bytes 4423684
  7.2 52.8 %collective-permute-start = (bf16[2,360,1440]{2,1,0:T(8,128)(2,1)}, bf16[2,360,1440]{2,1,0:T(8,128)(2,1)S(1)}, u32[]{:S(2)}, u32[]{:S(2)}) collective-permute-start(bf16[2,360,1440]{2,1,0:T(8,128)(2,1)} %param.11), channel_id=1, source_target_pairs={{0,24},{8,0},{16,8},{24,16},{1,25},{9,1},{17,9},{25,17},{2,26},{10... | collective-permute-start | bytes 6220808 | tf_op jit(solution)/shard_map/ppermute | solution.py:14
  60.0 4.9 copy-start.1
  64.9 192.6 %collective-permute-start.1 = (bf16[2,720,1440]{2,1,0:T(8,128)(2,1)}, bf16[2,720,1440]{2,1,0:T(8,128)(2,1)}, u32[]{:S(2)}, u32[]{:S(2)}) collective-permute-start(bf16[2,720,1440]{2,1,0:T(8,128)(2,1)} %pad_maximum_fusion), channel_id=1, source_target_pairs={{0,16},{8,24},{16,0},{24,8},{1,17},{9,25},{17,1},{25,9},{2,18},{10... | collective-permute-start | bytes 12441608 | tf_op jit(solution)/shard_map/ppermute | solution.py:14
  73.7 10.7 %all-to-all-start = ((bf16[8,1,80]{2,1,0:T(2,128)(2,1)}), bf16[8,1,80]{2,1,0:T(2,128)(2,1)S(1)}, u32[]{:S(2)}, u32[]{:S(2)}) async-start(bf16[8,1,80]{2,1,0:T(2,128)(2,1)} %all_to_all.25), calls=%async_computation | async-start | bytes 8192 | tf_op jit(solution)/shard_map/all_to_all | solution.py:49
  84.4 82.6 %copy-start.4 = (bf16[128,1440]{0,1:T(8,128)(2,1)S(1)}, bf16[128,1440]{0,1:T(8,128)(2,1)}, u32[]{:S(2)}) copy-start(bf16[128,1440]{0,1:T(8,128)(2,1)} %param.6) | copy-start | bytes 1105924
  84.4 94.8 %all-to-all-start.3 = ((bf16[8,80,1440]{2,1,0:T(8,128)(2,1)}), bf16[8,80,1440]{2,1,0:T(8,128)(2,1)}, u32[]{:S(2)}, u32[]{:S(2)}) async-start(bf16[8,80,1440]{2,1,0:T(8,128)(2,1)} %bitcast.12), calls=%async_computation.3 | async-start | bytes 3932160 | tf_op jit(solution)/shard_map/all_to_all | solution.py:51
  88.9 88.6 %copy-start = (bf16[2,360,1440]{2,1,0:T(8,128)(2,1)S(1)}, bf16[2,360,1440]{2,1,0:T(8,128)(2,1)}, u32[]{:S(2)}) copy-start(bf16[2,360,1440]{2,1,0:T(8,128)(2,1)} %param.11) | copy-start | bytes 6220804
  179.2 91.4 %all-to-all-start.1 = ((bf16[8,80,1440]{2,1,0:T(8,128)(2,1)}), bf16[8,80,1440]{2,1,0:T(8,128)(2,1)}, u32[]{:S(2)}, u32[]{:S(2)}) async-start(bf16[8,80,1440]{2,1,0:T(8,128)(2,1)} %bitcast.54), calls=%async_computation.1 | async-start | bytes 3932160 | tf_op jit(solution)/shard_map/all_to_all | solution.py:48
  183.5 442.8 %all-reduce.3.cloned.1.call-start = ((), (), s32[]{:S(2)}) async-start(), calls=%async_computation.5 | async-start | bytes 17694720
  262.1 2.4 copy-start.2
  291.9 8.3 %all-to-all-start.4 = ((bf16[8,1,80]{2,1,0:T(2,128)(2,1)}), bf16[8,1,80]{2,1,0:T(2,128)(2,1)S(1)}, u32[]{:S(2)}, u32[]{:S(2)}) async-start(bf16[8,1,80]{2,1,0:T(2,128)(2,1)} %convert_element_type.95), calls=%async_computation.4 | async-start | bytes 8192 | tf_op jit(solution)/shard_map/all_to_all | solution.py:75
  297.1 7.0 %copy-start.7 = (u32[32]{0:T(128)S(1)}, u32[32]{0:T(128)}, u32[]{:S(2)}) copy-start(u32[32]{0:T(128)} %constant.70) | copy-start | bytes 388
  300.2 28.8 %all-to-all-start.2 = ((bf16[8,80,1440]{2,1,0:T(8,128)(2,1)}), bf16[8,80,1440]{2,1,0:T(8,128)(2,1)S(1)}, u32[]{:S(2)}, u32[]{:S(2)}) async-start(bf16[8,80,1440]{2,1,0:T(8,128)(2,1)} %bitcast.55), calls=%async_computation.2 | async-start | bytes 3932160 | tf_op jit(solution)/shard_map/all_to_all | solution.py:68
Sparse Core Ops, SparseCore 0:
  291.3 334.8 all-reduce.2
